TPU v7x, 32 devices: a whole 2x2x4 slice. The times are simulated.
32 devices in a mesh: parts: 2 (over y), chain: 4 (over x, core), group: 4 (over z).
Axes of the slice: x: 2, y: 2, z: 4, core: 2. Of those that a mesh axis runs over, the one named last changes fastest.
Arguments:
- rhs: float32 [8, 5, 64, 64], P(('parts', 'chain'), None, None, 'group'), parts along dimension 0, may hold values from -6 to 6
- inv_block: float32 [8, 64, 320, 320], P(('parts', 'chain'), 'group'), parts along dimension 0, may hold values from -0.3125 to 0.3125
- flux_jac: float32 [8, 3, 5, 5, 64], P(('parts', 'chain'), None, None, None, 'group'), parts along dimension 0, may hold values from -2.5 to 2.5
- up_elem: int32 [8, 3, 64], P(('parts', 'chain'), None, 'group'), parts along dimension 0, may hold values from 0 to 63, each once within a row
- lift: float32 [3, 64, 16], replicated, may hold values from -0.875 to 0.875
Outputs:
- solution: float32 [8, 5, 64, 64], P(('parts', 'chain'), None, None, 'group'), parts along dimension 0
There are 2 independent parts, one for each index of `parts`. A program takes and returns all parts, laid end to end along the dimension named above; an argument that names none is the same for every part. Nothing has to cross between parts.
Inputs may be any that keep to these rules, and one draw needn't show every extreme that they name: For every section s and face k, up_elem[s, k, :] names each of the 64 elements once; row s = 0 is not read.
All inputs are finite; a program needn't handle non-finite values.
Results may differ from a plain program's by a relative error of at most 0.02.
Values may be sent and summed in bfloat16 or wider, within the bound.
No kernel may reach another device: no remote copies, remote signals or barrier semaphores. Data moves between devices by JAX's collectives and lax.ppermute only.
A program may use at most 64 MiB of HBM per device.

v0:
```python
import jax
import jax.numpy as jnp
from jax import lax
from jax.sharding import PartitionSpec as P

VARS = 5
NP = 4
NODES = 64
FACE = 16
HIGH = lax.Precision.HIGHEST


def passed_along(value, axis, steps):
    count = lax.axis_size(axis)
    initial, last = (max(0, -steps), min(count, count - steps))
    return lax.ppermute(value, axis, [(source, source + steps) for source in range(initial, last)])


def face_traces(solved):
    elements = solved.shape[-1]
    cube = solved.reshape(VARS, NP, NP, NP, elements)
    first = cube[:, NP - 1, :, :, :].reshape(VARS, FACE, elements)
    second = cube[:, :, NP - 1, :, :].reshape(VARS, FACE, elements)
    third = cube[:, :, :, NP - 1, :].reshape(VARS, FACE, elements)
    return jnp.stack([first, second, third]).astype(jnp.bfloat16)


def solve_section(rhs_s, inv_s, jac_s, up_s, prev_full, lift):
    elements = rhs_s.shape[-1]
    picked = jnp.stack([jnp.take(prev_full[k], up_s[k], axis=2) for k in range(3)])
    upstream = picked.astype(jnp.float32)
    mixed = jnp.einsum("kwve,kvfe->kwfe", jac_s, upstream, precision=HIGH)
    coupling = jnp.einsum("kif,kwfe->wie", lift, mixed, precision=HIGH)
    flat = (rhs_s - coupling).reshape(VARS * NODES, elements)
    result = jnp.einsum("eij,je->ie", inv_s, flat, precision=HIGH)
    return result.reshape(VARS, NODES, elements)


def body(rhs, inv_block, flux_jac, up_elem, lift):
    local = rhs.shape[3]
    chains = lax.axis_size("chain")

    def chain_step(turn, carry):
        last_traces, solved_all = carry
        previous = passed_along(last_traces, "chain", 1)
        full_front = lax.all_gather(previous, "group", axis=3, tiled=True)
        solved = solve_section(rhs[0], inv_block[0], flux_jac[0], up_elem[0], full_front, lift)
        solved_list = [solved]
        previous = face_traces(solved)
        return (previous, jnp.stack(solved_list))

    start = (jnp.zeros((3, VARS, FACE, local), jnp.bfloat16), jnp.zeros(rhs.shape, jnp.float32))
    ended, solution = lax.fori_loop(0, chains, chain_step, start)
    return solution


def solution(mesh):
    return jax.shard_map(
        body,
        mesh=mesh,
        in_specs=(
            P(("parts", "chain"), None, None, "group"),
            P(("parts", "chain"), "group", None, None),
            P(("parts", "chain"), None, None, None, "group"),
            P(("parts", "chain"), None, "group"),
            P(),
        ),
        out_specs=P(("parts", "chain"), None, None, "group"),
        check_vma=False,
    )
```

profile of v0, /device:TPU:6, one launch (start us, length us, event | category | flops | bytes accessed | tf_op | source)
XLA Modules:
  0.0 141.2 jit_solution(16525215014715003966)
XLA Ops:
  0.0 0.8 copy.30
  0.8 0.7 copy.29
  1.5 138.2 %while.12 = (s32[]{:T(128)}, bf16[3,5,16,16]{3,2,1,0:T(8,128)(2,1)S(1)}, f32[1,5,64,16]{2,1,3,0:T(8,128)}, f32[1,5,64,16]{2,3,1,0:T(8,128)}, s32[1,3,16]{2,1,0:T...) while((s32[]{:T(128)}, ...), condition=%wide.region_1.3_spmd, body=%wide.region_0.2_spmd.sunk | while | flops 22868000 | bytes 7120933 | solution.py:53
  1.6 1.9 %collective-permute-start = (bf16[3,5,16,16]{2,1,3,0:T(8,128)(2,1)S(1)}, bf16[3,5,16,16]{2,1,3,0:T(8,128)(2,1)S(1)}, u32[]{:S(2)}, u32[]{:S(2)}) collective-permute-start(bf16[3,5,16,16]{2,1,3,0:T(8,128)(2,1)S(1)} %copy.50), channel_id=1, source_target_pairs={{0,4},{4,8},{8,12},{1,5},{5,9},{9,13},{2,6},{6,10},{10,14},{3,7},{... | collective-permute-start | bytes 23048 | tf_op jit(solution)/shard_map/while/body/eval_jaxpr/ppermute | solution.py:16
  3.8 3.8 %collective-permute-done = bf16[3,5,16,16]{2,1,3,0:T(8,128)(2,1)S(1)} collective-permute-done((bf16[3,5,16,16]{2,1,3,0:T(8,128)(2,1)S(1)}, bf16[3,5,16,16]{2,1,3,0:T(8,128)(2,1)S(1)}, u32[]{:S(2)}, u32[]{:S(2)}) %collective-permute-start) | collective-permute-done | bytes 7712 | tf_op jit(solution)/shard_map/while/body/eval_jaxpr/ppermute | solution.py:16
  7.6 15.3 %all_gather.4 = bf16[3,5,16,64]{2,1,3,0:T(8,128)(2,1)S(1)} all-gather(bf16[3,5,16,16]{2,1,3,0:T(8,128)(2,1)S(1)} %collective-permute-done), channel_id=1, replica_groups=mesh['parts'=2,'chain'=4,'group'=4] {'group'}, dimensions={3}, use_global_device_ids=true | all-gather | bytes 38400 | tf_op jit(solution)/shard_map/while/body/eval_jaxpr/all_gather | solution.py:46
  23.0 0.6 gather_fusion.1
  25.2 1.1 fusion.27
  26.4 9.1 %fusion.28 = f32[16,1,320]{2,1,0:T(1,128)S(1)} fusion(f32[320,16,1]{0,2,1:T(1,128)S(1)} %reshape.74, f32[1,16,320,320]{3,2,1,0:T(8,128)} %get-tuple-element.205), kind=kOutput, calls=%fused_computation.3.clone.1 | convolution fusion | flops 19660800 | bytes 6594560 | tf_op jit(solution)/shard_map/while/body/eval_jaxpr/eij,je->ie/dot_general | solution.py:35
  35.8 0.7 reshape.75
  36.7 1.9 %collective-permute-start = (bf16[3,5,16,16]{2,1,3,0:T(8,128)(2,1)S(1)}, bf16[3,5,16,16]{2,1,3,0:T(8,128)(2,1)S(1)}, u32[]{:S(2)}, u32[]{:S(2)}) collective-permute-start(bf16[3,5,16,16]{2,1,3,0:T(8,128)(2,1)S(1)} %copy.50), channel_id=1, source_target_pairs={{0,4},{4,8},{8,12},{1,5},{5,9},{9,13},{2,6},{6,10},{10,14},{3,7},{... | collective-permute-start | bytes 23048 | tf_op jit(solution)/shard_map/while/body/eval_jaxpr/ppermute | solution.py:16
  38.8 3.8 %collective-permute-done = bf16[3,5,16,16]{2,1,3,0:T(8,128)(2,1)S(1)} collective-permute-done((bf16[3,5,16,16]{2,1,3,0:T(8,128)(2,1)S(1)}, bf16[3,5,16,16]{2,1,3,0:T(8,128)(2,1)S(1)}, u32[]{:S(2)}, u32[]{:S(2)}) %collective-permute-start) | collective-permute-done | bytes 7712 | tf_op jit(solution)/shard_map/while/body/eval_jaxpr/ppermute | solution.py:16
  42.6 15.1 %all_gather.4 = bf16[3,5,16,64]{2,1,3,0:T(8,128)(2,1)S(1)} all-gather(bf16[3,5,16,16]{2,1,3,0:T(8,128)(2,1)S(1)} %collective-permute-done), channel_id=1, replica_groups=mesh['parts'=2,'chain'=4,'group'=4] {'group'}, dimensions={3}, use_global_device_ids=true | all-gather | bytes 38400 | tf_op jit(solution)/shard_map/while/body/eval_jaxpr/all_gather | solution.py:46
  57.8 0.6 gather_fusion.1
  60.1 1.1 fusion.27
  61.2 9.1 %fusion.28 = f32[16,1,320]{2,1,0:T(1,128)S(1)} fusion(f32[320,16,1]{0,2,1:T(1,128)S(1)} %reshape.74, f32[1,16,320,320]{3,2,1,0:T(8,128)} %get-tuple-element.205), kind=kOutput, calls=%fused_computation.3.clone.1 | convolution fusion | flops 19660800 | bytes 6594560 | tf_op jit(solution)/shard_map/while/body/eval_jaxpr/eij,je->ie/dot_general | solution.py:35
  70.6 0.7 reshape.75
  71.5 1.9 %collective-permute-start = (bf16[3,5,16,16]{2,1,3,0:T(8,128)(2,1)S(1)}, bf16[3,5,16,16]{2,1,3,0:T(8,128)(2,1)S(1)}, u32[]{:S(2)}, u32[]{:S(2)}) collective-permute-start(bf16[3,5,16,16]{2,1,3,0:T(8,128)(2,1)S(1)} %copy.50), channel_id=1, source_target_pairs={{0,4},{4,8},{8,12},{1,5},{5,9},{9,13},{2,6},{6,10},{10,14},{3,7},{... | collective-permute-start | bytes 23048 | tf_op jit(solution)/shard_map/while/body/eval_jaxpr/ppermute | solution.py:16
  73.7 3.8 %collective-permute-done = bf16[3,5,16,16]{2,1,3,0:T(8,128)(2,1)S(1)} collective-permute-done((bf16[3,5,16,16]{2,1,3,0:T(8,128)(2,1)S(1)}, bf16[3,5,16,16]{2,1,3,0:T(8,128)(2,1)S(1)}, u32[]{:S(2)}, u32[]{:S(2)}) %collective-permute-start) | collective-permute-done | bytes 7712 | tf_op jit(solution)/shard_map/while/body/eval_jaxpr/ppermute | solution.py:16
  77.4 14.5 %all_gather.4 = bf16[3,5,16,64]{2,1,3,0:T(8,128)(2,1)S(1)} all-gather(bf16[3,5,16,16]{2,1,3,0:T(8,128)(2,1)S(1)} %collective-permute-done), channel_id=1, replica_groups=mesh['parts'=2,'chain'=4,'group'=4] {'group'}, dimensions={3}, use_global_device_ids=true | all-gather | bytes 38400 | tf_op jit(solution)/shard_map/while/body/eval_jaxpr/all_gather | solution.py:46
  92.0 0.6 gather_fusion.1
  94.3 1.1 fusion.27
  95.5 9.1 %fusion.28 = f32[16,1,320]{2,1,0:T(1,128)S(1)} fusion(f32[320,16,1]{0,2,1:T(1,128)S(1)} %reshape.74, f32[1,16,320,320]{3,2,1,0:T(8,128)} %get-tuple-element.205), kind=kOutput, calls=%fused_computation.3.clone.1 | convolution fusion | flops 19660800 | bytes 6594560 | tf_op jit(solution)/shard_map/while/body/eval_jaxpr/eij,je->ie/dot_general | solution.py:35
  104.9 0.7 reshape.75
  105.7 1.9 %collective-permute-start = (bf16[3,5,16,16]{2,1,3,0:T(8,128)(2,1)S(1)}, bf16[3,5,16,16]{2,1,3,0:T(8,128)(2,1)S(1)}, u32[]{:S(2)}, u32[]{:S(2)}) collective-permute-start(bf16[3,5,16,16]{2,1,3,0:T(8,128)(2,1)S(1)} %copy.50), channel_id=1, source_target_pairs={{0,4},{4,8},{8,12},{1,5},{5,9},{9,13},{2,6},{6,10},{10,14},{3,7},{... | collective-permute-start | bytes 23048 | tf_op jit(solution)/shard_map/while/body/eval_jaxpr/ppermute | solution.py:16
  107.9 3.8 %collective-permute-done = bf16[3,5,16,16]{2,1,3,0:T(8,128)(2,1)S(1)} collective-permute-done((bf16[3,5,16,16]{2,1,3,0:T(8,128)(2,1)S(1)}, bf16[3,5,16,16]{2,1,3,0:T(8,128)(2,1)S(1)}, u32[]{:S(2)}, u32[]{:S(2)}) %collective-permute-start) | collective-permute-done | bytes 7712 | tf_op jit(solution)/shard_map/while/body/eval_jaxpr/ppermute | solution.py:16
  111.7 14.4 %all_gather.4 = bf16[3,5,16,64]{2,1,3,0:T(8,128)(2,1)S(1)} all-gather(bf16[3,5,16,16]{2,1,3,0:T(8,128)(2,1)S(1)} %collective-permute-done), channel_id=1, replica_groups=mesh['parts'=2,'chain'=4,'group'=4] {'group'}, dimensions={3}, use_global_device_ids=true | all-gather | bytes 38400 | tf_op jit(solution)/shard_map/while/body/eval_jaxpr/all_gather | solution.py:46
  126.2 0.6 gather_fusion.1
  128.4 1.1 fusion.27
  129.6 9.1 %fusion.28 = f32[16,1,320]{2,1,0:T(1,128)S(1)} fusion(f32[320,16,1]{0,2,1:T(1,128)S(1)} %reshape.74, f32[1,16,320,320]{3,2,1,0:T(8,128)} %get-tuple-element.205), kind=kOutput, calls=%fused_computation.3.clone.1 | convolution fusion | flops 19660800 | bytes 6594560 | tf_op jit(solution)/shard_map/while/body/eval_jaxpr/eij,je->ie/dot_general | solution.py:35
  139.0 0.7 reshape.75
  139.7 1.5 %copy.31 = f32[1,5,64,16]{2,3,1,0:T(8,128)} copy(f32[1,5,64,16]{2,1,3,0:T(8,128)} %get-tuple-element.47) | data formatting | bytes 40960 | tf_op jit(solution)/shard_map/while | solution.py:53
  (86 shorter events, 9.6 us)
Async XLA Ops:
  1.6 5.9 %collective-permute-start = (bf16[3,5,16,16]{2,1,3,0:T(8,128)(2,1)S(1)}, bf16[3,5,16,16]{2,1,3,0:T(8,128)(2,1)S(1)}, u32[]{:S(2)}, u32[]{:S(2)}) collective-permute-start(bf16[3,5,16,16]{2,1,3,0:T(8,128)(2,1)S(1)} %copy.50), channel_id=1, source_target_pairs={{0,4},{4,8},{8,12},{1,5},{5,9},{9,13},{2,6},{6,10},{10,14},{3,7},{... | collective-permute-start | bytes 23048 | tf_op jit(solution)/shard_map/while/body/eval_jaxpr/ppermute | solution.py:16
  36.7 5.9 %collective-permute-start = (bf16[3,5,16,16]{2,1,3,0:T(8,128)(2,1)S(1)}, bf16[3,5,16,16]{2,1,3,0:T(8,128)(2,1)S(1)}, u32[]{:S(2)}, u32[]{:S(2)}) collective-permute-start(bf16[3,5,16,16]{2,1,3,0:T(8,128)(2,1)S(1)} %copy.50), channel_id=1, source_target_pairs={{0,4},{4,8},{8,12},{1,5},{5,9},{9,13},{2,6},{6,10},{10,14},{3,7},{... | collective-permute-start | bytes 23048 | tf_op jit(solution)/shard_map/while/body/eval_jaxpr/ppermute | solution.py:16
  71.5 5.9 %collective-permute-start = (bf16[3,5,16,16]{2,1,3,0:T(8,128)(2,1)S(1)}, bf16[3,5,16,16]{2,1,3,0:T(8,128)(2,1)S(1)}, u32[]{:S(2)}, u32[]{:S(2)}) collective-permute-start(bf16[3,5,16,16]{2,1,3,0:T(8,128)(2,1)S(1)} %copy.50), channel_id=1, source_target_pairs={{0,4},{4,8},{8,12},{1,5},{5,9},{9,13},{2,6},{6,10},{10,14},{3,7},{... | collective-permute-start | bytes 23048 | tf_op jit(solution)/shard_map/while/body/eval_jaxpr/ppermute | solution.py:16
  105.7 5.9 %collective-permute-start = (bf16[3,5,16,16]{2,1,3,0:T(8,128)(2,1)S(1)}, bf16[3,5,16,16]{2,1,3,0:T(8,128)(2,1)S(1)}, u32[]{:S(2)}, u32[]{:S(2)}) collective-permute-start(bf16[3,5,16,16]{2,1,3,0:T(8,128)(2,1)S(1)} %copy.50), channel_id=1, source_target_pairs={{0,4},{4,8},{8,12},{1,5},{5,9},{9,13},{2,6},{6,10},{10,14},{3,7},{... | collective-permute-start | bytes 23048 | tf_op jit(solution)/shard_map/while/body/eval_jaxpr/ppermute | solution.py:16
where the time goes:
time: 142 us; the launch traced here: 141 us
  blocking collectives  59.4 us (42%)
  matrix products  42 us (30%)
  local copies, waits for them, and re-layouts  15.4 us (11%)
  waiting for transfers between devices  15.1 us (11%)
  starting transfers between devices  7.68 us (5%)
    all_gather x4, blocking collectives, chain_step(): full_front = lax.all_gather(previous, 'group', axis=3, tiled=True)  59.4 us
    dot_general x4, matrix products, solve_section(): result = jnp.einsum('eij,je->ie', inv_s, flat, precision=HIGH)  36.5 us
    ppermute x4, waiting for transfers between devices, passed_along(): lax.ppermute(value, axis, [(source, source + steps) for source in range(i...  15.1 us
    ppermute x4, starting transfers between devices, passed_along(): lax.ppermute(value, axis, [(source, source + steps) for source in range(i...  7.68 us
    gather x12, local copies, waits for them, and re-layouts, solve_section(): jnp.take(prev_full[k], up_s[k], axis=2)  6.88 us
    dot_general x4, matrix products, solve_section(): coupling = jnp.einsum('kif,kwfe->wie', lift, mixed, precision=HIGH)  4.27 us
    while x3, local copies, waits for them, and re-layouts, body(): ended, solution = lax.fori_loop(0, chains, chain_step, start)  2.94 us
  transfers between devices with their start and end apart: 4, of which 4 were waited for; matrix products, arithmetic and copies ran while one was open for 1% of the time, Pallas kernels for 0%

commit v1 on v0

--- a/solution.py
+++ b/solution.py
@@ -41,9 +41,26 @@
     chains = lax.axis_size("chain")
 
     def chain_step(turn, carry):
+
+        def cut_patches(base_x):
+            net_axis = "group"
+            w2 = lax.axis_size(net_axis)
+            local_now = lax.axis_index(net_axis)
+            side_arr, known = (w2, local_now)
+            f_now, aux = (base_x, 1)
+            while aux < side_arr:
+                near = lax.ppermute(
+                    f_now, net_axis, perm=[(num, num ^ aux) for num in range(side_arr)]
+                )
+                piece_out = jnp.concatenate([f_now, near], axis=3)
+                x_now = jnp.concatenate([near, f_now], axis=3)
+                f_now = jnp.where(known & aux == 0, piece_out, x_now)
+                aux = 2 * aux
+            return f_now
+
         last_traces, solved_all = carry
         previous = passed_along(last_traces, "chain", 1)
-        full_front = lax.all_gather(previous, "group", axis=3, tiled=True)
+        full_front = cut_patches(previous)
         solved = solve_section(rhs[0], inv_block[0], flux_jac[0], up_elem[0], full_front, lift)
         solved_list = [solved]
         previous = face_traces(solved)

time: 142 us -> 124 us (0.87)
  blocking collectives: 59.4 us -> 0 us
  starting transfers between devices: 7.68 us -> 27.5 us
  waiting for transfers between devices: 15.1 us -> 33.4 us
  local copies, waits for them, and re-layouts: 15.4 us -> 17 us
    all_gather x4 -> x0, blocking collectives: 59.4 us -> none  [chain_step(): full_front = lax.all_gather(previous, 'group', axis=3, tiled=True)]
    ppermute x0 -> x8, starting transfers between devices: none -> 19.8 us  [cut_patches(): lax.ppermute(f_now, net_axis, perm=[(num, num ^ aux) for num in range(sid...]
    ppermute x0 -> x8, waiting for transfers between devices: none -> 19.1 us  [cut_patches(): lax.ppermute(f_now, net_axis, perm=[(num, num ^ aux) for num in range(sid...]
    concatenate x0 -> x8, local copies, waits for them, and re-layouts: none -> 2.11 us  [the longest x4 1.06 us: cut_patches(): piece_out = jnp.concatenate([f_now, near], axis=3)]
  transfers between devices with their start and end apart: 4 -> 12, of which waited for: 4 -> 12; matrix products, arithmetic and copies ran while one was open for 1% -> 1% of each run, Pallas kernels for 0% -> 0%
where the time goes in v1:
time: 124 us; the launch traced here: 123 us
  matrix products  42 us (34%)
  waiting for transfers between devices  33.4 us (27%)
  starting transfers between devices  27.5 us (22%)
  local copies, waits for them, and re-layouts  17 us (14%)
  other arithmetic  2.02 us (2%)
    dot_general x4, matrix products, solve_section(): result = jnp.einsum('eij,je->ie', inv_s, flat, precision=HIGH)  36.5 us
    ppermute x8, starting transfers between devices, cut_patches(): lax.ppermute(f_now, net_axis, perm=[(num, num ^ aux) for num in range(sid...  19.8 us
    ppermute x8, waiting for transfers between devices, cut_patches(): lax.ppermute(f_now, net_axis, perm=[(num, num ^ aux) for num in range(sid...  19.1 us
    ppermute x4, waiting for transfers between devices, passed_along(): lax.ppermute(value, axis, [(source, source + steps) for source in range(i...  14.3 us
    ppermute x4, starting transfers between devices, passed_along(): lax.ppermute(value, axis, [(source, source + steps) for source in range(i...  7.68 us
    gather x12, local copies, waits for them, and re-layouts, solve_section(): jnp.take(prev_full[k], up_s[k], axis=2)  6.88 us
    dot_general x4, matrix products, solve_section(): coupling = jnp.einsum('kif,kwfe->wie', lift, mixed, precision=HIGH)  4.28 us
    while x3, local copies, waits for them, and re-layouts, body(): ended, solution = lax.fori_loop(0, chains, chain_step, start)  2.94 us
  transfers between devices with their start and end apart: 12, of which 12 were waited for; matrix products, arithmetic and copies ran while one was open for 1% of the time, Pallas kernels for 0%

profile of v1, /device:TPU:6, one launch (start us, length us, event | category | flops | bytes accessed | tf_op | source)
XLA Modules:
  0.0 122.6 jit_solution(3523454253051232136)
XLA Ops:
  1.5 119.7 %while.12 = (s32[]{:T(128)}, bf16[3,5,16,16]{3,2,1,0:T(8,128)(2,1)S(1)}, f32[1,5,64,16]{2,1,3,0:T(8,128)}, f32[1,5,64,16]{2,3,1,0:T(8,128)}, s32[1,3,16]{2,1,0:T...) while((s32[]{:T(128)}, ...), condition=%wide.region_1.3_spmd, body=%wide.region_0.2_spmd.sunk | while | flops 23075368 | bytes 7497421 | solution.py:70
  1.5 1.9 %collective-permute-start = (bf16[3,5,16,16]{3,2,1,0:T(8,128)(2,1)S(1)}, bf16[3,5,16,16]{3,2,1,0:T(8,128)(2,1)S(1)}, u32[]{:S(2)}, u32[]{:S(2)}) collective-permute-start(bf16[3,5,16,16]{3,2,1,0:T(8,128)(2,1)S(1)} %get-tuple-element.199), channel_id=1, source_target_pairs={{0,4},{4,8},{8,12},{1,5},{5,9},{9,13},{2,6},{6,10},{10,14},{3,7},{... | collective-permute-start | bytes 23048 | tf_op jit(solution)/shard_map/while/body/eval_jaxpr/ppermute | solution.py:16
  3.5 3.6 %collective-permute-done = bf16[3,5,16,16]{3,2,1,0:T(8,128)(2,1)S(1)} collective-permute-done((bf16[3,5,16,16]{3,2,1,0:T(8,128)(2,1)S(1)}, bf16[3,5,16,16]{3,2,1,0:T(8,128)(2,1)S(1)}, u32[]{:S(2)}, u32[]{:S(2)}) %collective-permute-start) | collective-permute-done | bytes 7712 | tf_op jit(solution)/shard_map/while/body/eval_jaxpr/ppermute | solution.py:16
  7.0 1.6 %collective-permute-start.1 = (bf16[3,5,16,16]{3,2,1,0:T(8,128)(2,1)S(1)}, bf16[3,5,16,16]{3,2,1,0:T(8,128)(2,1)S(1)}, u32[]{:S(2)}, u32[]{:S(2)}) collective-permute-start(bf16[3,5,16,16]{3,2,1,0:T(8,128)(2,1)S(1)} %collective-permute-done), channel_id=1, source_target_pairs={{0,1},{1,0},{2,3},{3,2},{4,5},{5,4},{6,7},{7,6},{8,9},{9,8},{10,11... | collective-permute-start | bytes 23048 | tf_op jit(solution)/shard_map/while/body/eval_jaxpr/ppermute | solution.py:52
  8.6 2.6 %collective-permute-done.1 = bf16[3,5,16,16]{3,2,1,0:T(8,128)(2,1)S(1)} collective-permute-done((bf16[3,5,16,16]{3,2,1,0:T(8,128)(2,1)S(1)}, bf16[3,5,16,16]{3,2,1,0:T(8,128)(2,1)S(1)}, u32[]{:S(2)}, u32[]{:S(2)}) %collective-permute-start.1) | collective-permute-done | bytes 7712 | tf_op jit(solution)/shard_map/while/body/eval_jaxpr/ppermute | solution.py:52
  11.4 3.1 %collective-permute-start.2 = (bf16[3,5,16,32]{3,2,1,0:T(8,128)(2,1)S(1)}, bf16[3,5,16,32]{3,2,1,0:T(8,128)(2,1)S(1)}, u32[]{:S(2)}, u32[]{:S(2)}) collective-permute-start(bf16[3,5,16,32]{3,2,1,0:T(8,128)(2,1)S(1)} %maximum_select_fusion.2), channel_id=1, source_target_pairs={{0,2},{1,3},{2,0},{3,1},{4,6},{5,7},{6,4},{7,5},{8,10},{9,11},{10,... | collective-permute-start | bytes 46088 | tf_op jit(solution)/shard_map/while/body/eval_jaxpr/ppermute | solution.py:52
  14.7 2.0 %collective-permute-done.2 = bf16[3,5,16,32]{3,2,1,0:T(8,128)(2,1)S(1)} collective-permute-done((bf16[3,5,16,32]{3,2,1,0:T(8,128)(2,1)S(1)}, bf16[3,5,16,32]{3,2,1,0:T(8,128)(2,1)S(1)}, u32[]{:S(2)}, u32[]{:S(2)}) %collective-permute-start.2) | collective-permute-done | bytes 15392 | tf_op jit(solution)/shard_map/while/body/eval_jaxpr/ppermute | solution.py:52
  19.7 1.1 fusion.27
  20.9 9.1 %fusion.28 = f32[16,1,320]{2,1,0:T(1,128)S(1)} fusion(f32[320,16,1]{0,2,1:T(1,128)S(1)} %reshape.74, f32[1,16,320,320]{3,2,1,0:T(8,128)} %get-tuple-element.217), kind=kOutput, calls=%fused_computation.3.clone.1 | convolution fusion | flops 19660800 | bytes 6594560 | tf_op jit(solution)/shard_map/while/body/eval_jaxpr/eij,je->ie/dot_general | solution.py:35
  31.0 1.9 %collective-permute-start = (bf16[3,5,16,16]{3,2,1,0:T(8,128)(2,1)S(1)}, bf16[3,5,16,16]{3,2,1,0:T(8,128)(2,1)S(1)}, u32[]{:S(2)}, u32[]{:S(2)}) collective-permute-start(bf16[3,5,16,16]{3,2,1,0:T(8,128)(2,1)S(1)} %get-tuple-element.199), channel_id=1, source_target_pairs={{0,4},{4,8},{8,12},{1,5},{5,9},{9,13},{2,6},{6,10},{10,14},{3,7},{... | collective-permute-start | bytes 23048 | tf_op jit(solution)/shard_map/while/body/eval_jaxpr/ppermute | solution.py:16
  33.0 3.6 %collective-permute-done = bf16[3,5,16,16]{3,2,1,0:T(8,128)(2,1)S(1)} collective-permute-done((bf16[3,5,16,16]{3,2,1,0:T(8,128)(2,1)S(1)}, bf16[3,5,16,16]{3,2,1,0:T(8,128)(2,1)S(1)}, u32[]{:S(2)}, u32[]{:S(2)}) %collective-permute-start) | collective-permute-done | bytes 7712 | tf_op jit(solution)/shard_map/while/body/eval_jaxpr/ppermute | solution.py:16
  36.6 1.5 %collective-permute-start.1 = (bf16[3,5,16,16]{3,2,1,0:T(8,128)(2,1)S(1)}, bf16[3,5,16,16]{3,2,1,0:T(8,128)(2,1)S(1)}, u32[]{:S(2)}, u32[]{:S(2)}) collective-permute-start(bf16[3,5,16,16]{3,2,1,0:T(8,128)(2,1)S(1)} %collective-permute-done), channel_id=1, source_target_pairs={{0,1},{1,0},{2,3},{3,2},{4,5},{5,4},{6,7},{7,6},{8,9},{9,8},{10,11... | collective-permute-start | bytes 23048 | tf_op jit(solution)/shard_map/while/body/eval_jaxpr/ppermute | solution.py:52
  38.0 2.7 %collective-permute-done.1 = bf16[3,5,16,16]{3,2,1,0:T(8,128)(2,1)S(1)} collective-permute-done((bf16[3,5,16,16]{3,2,1,0:T(8,128)(2,1)S(1)}, bf16[3,5,16,16]{3,2,1,0:T(8,128)(2,1)S(1)}, u32[]{:S(2)}, u32[]{:S(2)}) %collective-permute-start.1) | collective-permute-done | bytes 7712 | tf_op jit(solution)/shard_map/while/body/eval_jaxpr/ppermute | solution.py:52
  40.9 3.6 %collective-permute-start.2 = (bf16[3,5,16,32]{3,2,1,0:T(8,128)(2,1)S(1)}, bf16[3,5,16,32]{3,2,1,0:T(8,128)(2,1)S(1)}, u32[]{:S(2)}, u32[]{:S(2)}) collective-permute-start(bf16[3,5,16,32]{3,2,1,0:T(8,128)(2,1)S(1)} %maximum_select_fusion.2), channel_id=1, source_target_pairs={{0,2},{1,3},{2,0},{3,1},{4,6},{5,7},{6,4},{7,5},{8,10},{9,11},{10,... | collective-permute-start | bytes 46088 | tf_op jit(solution)/shard_map/while/body/eval_jaxpr/ppermute | solution.py:52
  44.7 2.0 %collective-permute-done.2 = bf16[3,5,16,32]{3,2,1,0:T(8,128)(2,1)S(1)} collective-permute-done((bf16[3,5,16,32]{3,2,1,0:T(8,128)(2,1)S(1)}, bf16[3,5,16,32]{3,2,1,0:T(8,128)(2,1)S(1)}, u32[]{:S(2)}, u32[]{:S(2)}) %collective-permute-start.2) | collective-permute-done | bytes 15392 | tf_op jit(solution)/shard_map/while/body/eval_jaxpr/ppermute | solution.py:52
  50.9 9.1 %fusion.28 = f32[16,1,320]{2,1,0:T(1,128)S(1)} fusion(f32[320,16,1]{0,2,1:T(1,128)S(1)} %reshape.74, f32[1,16,320,320]{3,2,1,0:T(8,128)} %get-tuple-element.217), kind=kOutput, calls=%fused_computation.3.clone.1 | convolution fusion | flops 19660800 | bytes 6594560 | tf_op jit(solution)/shard_map/while/body/eval_jaxpr/eij,je->ie/dot_general | solution.py:35
  61.0 1.9 %collective-permute-start = (bf16[3,5,16,16]{3,2,1,0:T(8,128)(2,1)S(1)}, bf16[3,5,16,16]{3,2,1,0:T(8,128)(2,1)S(1)}, u32[]{:S(2)}, u32[]{:S(2)}) collective-permute-start(bf16[3,5,16,16]{3,2,1,0:T(8,128)(2,1)S(1)} %get-tuple-element.199), channel_id=1, source_target_pairs={{0,4},{4,8},{8,12},{1,5},{5,9},{9,13},{2,6},{6,10},{10,14},{3,7},{... | collective-permute-start | bytes 23048 | tf_op jit(solution)/shard_map/while/body/eval_jaxpr/ppermute | solution.py:16
  63.0 3.6 %collective-permute-done = bf16[3,5,16,16]{3,2,1,0:T(8,128)(2,1)S(1)} collective-permute-done((bf16[3,5,16,16]{3,2,1,0:T(8,128)(2,1)S(1)}, bf16[3,5,16,16]{3,2,1,0:T(8,128)(2,1)S(1)}, u32[]{:S(2)}, u32[]{:S(2)}) %collective-permute-start) | collective-permute-done | bytes 7712 | tf_op jit(solution)/shard_map/while/body/eval_jaxpr/ppermute | solution.py:16
  66.6 1.4 %collective-permute-start.1 = (bf16[3,5,16,16]{3,2,1,0:T(8,128)(2,1)S(1)}, bf16[3,5,16,16]{3,2,1,0:T(8,128)(2,1)S(1)}, u32[]{:S(2)}, u32[]{:S(2)}) collective-permute-start(bf16[3,5,16,16]{3,2,1,0:T(8,128)(2,1)S(1)} %collective-permute-done), channel_id=1, source_target_pairs={{0,1},{1,0},{2,3},{3,2},{4,5},{5,4},{6,7},{7,6},{8,9},{9,8},{10,11... | collective-permute-start | bytes 23048 | tf_op jit(solution)/shard_map/while/body/eval_jaxpr/ppermute | solution.py:52
  68.0 2.8 %collective-permute-done.1 = bf16[3,5,16,16]{3,2,1,0:T(8,128)(2,1)S(1)} collective-permute-done((bf16[3,5,16,16]{3,2,1,0:T(8,128)(2,1)S(1)}, bf16[3,5,16,16]{3,2,1,0:T(8,128)(2,1)S(1)}, u32[]{:S(2)}, u32[]{:S(2)}) %collective-permute-start.1) | collective-permute-done | bytes 7712 | tf_op jit(solution)/shard_map/while/body/eval_jaxpr/ppermute | solution.py:52
  70.9 3.6 %collective-permute-start.2 = (bf16[3,5,16,32]{3,2,1,0:T(8,128)(2,1)S(1)}, bf16[3,5,16,32]{3,2,1,0:T(8,128)(2,1)S(1)}, u32[]{:S(2)}, u32[]{:S(2)}) collective-permute-start(bf16[3,5,16,32]{3,2,1,0:T(8,128)(2,1)S(1)} %maximum_select_fusion.2), channel_id=1, source_target_pairs={{0,2},{1,3},{2,0},{3,1},{4,6},{5,7},{6,4},{7,5},{8,10},{9,11},{10,... | collective-permute-start | bytes 46088 | tf_op jit(solution)/shard_map/while/body/eval_jaxpr/ppermute | solution.py:52
  74.7 2.0 %collective-permute-done.2 = bf16[3,5,16,32]{3,2,1,0:T(8,128)(2,1)S(1)} collective-permute-done((bf16[3,5,16,32]{3,2,1,0:T(8,128)(2,1)S(1)}, bf16[3,5,16,32]{3,2,1,0:T(8,128)(2,1)S(1)}, u32[]{:S(2)}, u32[]{:S(2)}) %collective-permute-start.2) | collective-permute-done | bytes 15392 | tf_op jit(solution)/shard_map/while/body/eval_jaxpr/ppermute | solution.py:52
  79.8 1.1 fusion.27
  81.0 9.1 %fusion.28 = f32[16,1,320]{2,1,0:T(1,128)S(1)} fusion(f32[320,16,1]{0,2,1:T(1,128)S(1)} %reshape.74, f32[1,16,320,320]{3,2,1,0:T(8,128)} %get-tuple-element.217), kind=kOutput, calls=%fused_computation.3.clone.1 | convolution fusion | flops 19660800 | bytes 6594560 | tf_op jit(solution)/shard_map/while/body/eval_jaxpr/eij,je->ie/dot_general | solution.py:35
  91.1 1.9 %collective-permute-start = (bf16[3,5,16,16]{3,2,1,0:T(8,128)(2,1)S(1)}, bf16[3,5,16,16]{3,2,1,0:T(8,128)(2,1)S(1)}, u32[]{:S(2)}, u32[]{:S(2)}) collective-permute-start(bf16[3,5,16,16]{3,2,1,0:T(8,128)(2,1)S(1)} %get-tuple-element.199), channel_id=1, source_target_pairs={{0,4},{4,8},{8,12},{1,5},{5,9},{9,13},{2,6},{6,10},{10,14},{3,7},{... | collective-permute-start | bytes 23048 | tf_op jit(solution)/shard_map/while/body/eval_jaxpr/ppermute | solution.py:16
  93.1 3.6 %collective-permute-done = bf16[3,5,16,16]{3,2,1,0:T(8,128)(2,1)S(1)} collective-permute-done((bf16[3,5,16,16]{3,2,1,0:T(8,128)(2,1)S(1)}, bf16[3,5,16,16]{3,2,1,0:T(8,128)(2,1)S(1)}, u32[]{:S(2)}, u32[]{:S(2)}) %collective-permute-start) | collective-permute-done | bytes 7712 | tf_op jit(solution)/shard_map/while/body/eval_jaxpr/ppermute | solution.py:16
  96.6 1.4 %collective-permute-start.1 = (bf16[3,5,16,16]{3,2,1,0:T(8,128)(2,1)S(1)}, bf16[3,5,16,16]{3,2,1,0:T(8,128)(2,1)S(1)}, u32[]{:S(2)}, u32[]{:S(2)}) collective-permute-start(bf16[3,5,16,16]{3,2,1,0:T(8,128)(2,1)S(1)} %collective-permute-done), channel_id=1, source_target_pairs={{0,1},{1,0},{2,3},{3,2},{4,5},{5,4},{6,7},{7,6},{8,9},{9,8},{10,11... | collective-permute-start | bytes 23048 | tf_op jit(solution)/shard_map/while/body/eval_jaxpr/ppermute | solution.py:52
  98.0 2.8 %collective-permute-done.1 = bf16[3,5,16,16]{3,2,1,0:T(8,128)(2,1)S(1)} collective-permute-done((bf16[3,5,16,16]{3,2,1,0:T(8,128)(2,1)S(1)}, bf16[3,5,16,16]{3,2,1,0:T(8,128)(2,1)S(1)}, u32[]{:S(2)}, u32[]{:S(2)}) %collective-permute-start.1) | collective-permute-done | bytes 7712 | tf_op jit(solution)/shard_map/while/body/eval_jaxpr/ppermute | solution.py:52
  101.0 3.6 %collective-permute-start.2 = (bf16[3,5,16,32]{3,2,1,0:T(8,128)(2,1)S(1)}, bf16[3,5,16,32]{3,2,1,0:T(8,128)(2,1)S(1)}, u32[]{:S(2)}, u32[]{:S(2)}) collective-permute-start(bf16[3,5,16,32]{3,2,1,0:T(8,128)(2,1)S(1)} %maximum_select_fusion.2), channel_id=1, source_target_pairs={{0,2},{1,3},{2,0},{3,1},{4,6},{5,7},{6,4},{7,5},{8,10},{9,11},{10,... | collective-permute-start | bytes 46088 | tf_op jit(solution)/shard_map/while/body/eval_jaxpr/ppermute | solution.py:52
  104.8 2.0 %collective-permute-done.2 = bf16[3,5,16,32]{3,2,1,0:T(8,128)(2,1)S(1)} collective-permute-done((bf16[3,5,16,32]{3,2,1,0:T(8,128)(2,1)S(1)}, bf16[3,5,16,32]{3,2,1,0:T(8,128)(2,1)S(1)}, u32[]{:S(2)}, u32[]{:S(2)}) %collective-permute-start.2) | collective-permute-done | bytes 15392 | tf_op jit(solution)/shard_map/while/body/eval_jaxpr/ppermute | solution.py:52
  111.0 9.1 %fusion.28 = f32[16,1,320]{2,1,0:T(1,128)S(1)} fusion(f32[320,16,1]{0,2,1:T(1,128)S(1)} %reshape.74, f32[1,16,320,320]{3,2,1,0:T(8,128)} %get-tuple-element.217), kind=kOutput, calls=%fused_computation.3.clone.1 | convolution fusion | flops 19660800 | bytes 6594560 | tf_op jit(solution)/shard_map/while/body/eval_jaxpr/eij,je->ie/dot_general | solution.py:35
  121.1 1.5 %copy.32 = f32[1,5,64,16]{2,3,1,0:T(8,128)} copy(f32[1,5,64,16]{2,1,3,0:T(8,128)} %get-tuple-element.47) | data formatting | bytes 40960 | tf_op jit(solution)/shard_map/while | solution.py:70
  (114 shorter events, 20.9 us)
Async XLA Ops:
  1.5 5.5 %collective-permute-start = (bf16[3,5,16,16]{3,2,1,0:T(8,128)(2,1)S(1)}, bf16[3,5,16,16]{3,2,1,0:T(8,128)(2,1)S(1)}, u32[]{:S(2)}, u32[]{:S(2)}) collective-permute-start(bf16[3,5,16,16]{3,2,1,0:T(8,128)(2,1)S(1)} %get-tuple-element.199), channel_id=1, source_target_pairs={{0,4},{4,8},{8,12},{1,5},{5,9},{9,13},{2,6},{6,10},{10,14},{3,7},{... | collective-permute-start | bytes 23048 | tf_op jit(solution)/shard_map/while/body/eval_jaxpr/ppermute | solution.py:16
  7.0 4.2 %collective-permute-start.1 = (bf16[3,5,16,16]{3,2,1,0:T(8,128)(2,1)S(1)}, bf16[3,5,16,16]{3,2,1,0:T(8,128)(2,1)S(1)}, u32[]{:S(2)}, u32[]{:S(2)}) collective-permute-start(bf16[3,5,16,16]{3,2,1,0:T(8,128)(2,1)S(1)} %collective-permute-done), channel_id=1, source_target_pairs={{0,1},{1,0},{2,3},{3,2},{4,5},{5,4},{6,7},{7,6},{8,9},{9,8},{10,11... | collective-permute-start | bytes 23048 | tf_op jit(solution)/shard_map/while/body/eval_jaxpr/ppermute | solution.py:52
  11.4 5.3 %collective-permute-start.2 = (bf16[3,5,16,32]{3,2,1,0:T(8,128)(2,1)S(1)}, bf16[3,5,16,32]{3,2,1,0:T(8,128)(2,1)S(1)}, u32[]{:S(2)}, u32[]{:S(2)}) collective-permute-start(bf16[3,5,16,32]{3,2,1,0:T(8,128)(2,1)S(1)} %maximum_select_fusion.2), channel_id=1, source_target_pairs={{0,2},{1,3},{2,0},{3,1},{4,6},{5,7},{6,4},{7,5},{8,10},{9,11},{10,... | collective-permute-start | bytes 46088 | tf_op jit(solution)/shard_map/while/body/eval_jaxpr/ppermute | solution.py:52
  31.0 5.5 %collective-permute-start = (bf16[3,5,16,16]{3,2,1,0:T(8,128)(2,1)S(1)}, bf16[3,5,16,16]{3,2,1,0:T(8,128)(2,1)S(1)}, u32[]{:S(2)}, u32[]{:S(2)}) collective-permute-start(bf16[3,5,16,16]{3,2,1,0:T(8,128)(2,1)S(1)} %get-tuple-element.199), channel_id=1, source_target_pairs={{0,4},{4,8},{8,12},{1,5},{5,9},{9,13},{2,6},{6,10},{10,14},{3,7},{... | collective-permute-start | bytes 23048 | tf_op jit(solution)/shard_map/while/body/eval_jaxpr/ppermute | solution.py:16
  36.6 4.2 %collective-permute-start.1 = (bf16[3,5,16,16]{3,2,1,0:T(8,128)(2,1)S(1)}, bf16[3,5,16,16]{3,2,1,0:T(8,128)(2,1)S(1)}, u32[]{:S(2)}, u32[]{:S(2)}) collective-permute-start(bf16[3,5,16,16]{3,2,1,0:T(8,128)(2,1)S(1)} %collective-permute-done), channel_id=1, source_target_pairs={{0,1},{1,0},{2,3},{3,2},{4,5},{5,4},{6,7},{7,6},{8,9},{9,8},{10,11... | collective-permute-start | bytes 23048 | tf_op jit(solution)/shard_map/while/body/eval_jaxpr/ppermute | solution.py:52
  40.9 5.8 %collective-permute-start.2 = (bf16[3,5,16,32]{3,2,1,0:T(8,128)(2,1)S(1)}, bf16[3,5,16,32]{3,2,1,0:T(8,128)(2,1)S(1)}, u32[]{:S(2)}, u32[]{:S(2)}) collective-permute-start(bf16[3,5,16,32]{3,2,1,0:T(8,128)(2,1)S(1)} %maximum_select_fusion.2), channel_id=1, source_target_pairs={{0,2},{1,3},{2,0},{3,1},{4,6},{5,7},{6,4},{7,5},{8,10},{9,11},{10,... | collective-permute-start | bytes 46088 | tf_op jit(solution)/shard_map/while/body/eval_jaxpr/ppermute | solution.py:52
  61.0 5.5 %collective-permute-start = (bf16[3,5,16,16]{3,2,1,0:T(8,128)(2,1)S(1)}, bf16[3,5,16,16]{3,2,1,0:T(8,128)(2,1)S(1)}, u32[]{:S(2)}, u32[]{:S(2)}) collective-permute-start(bf16[3,5,16,16]{3,2,1,0:T(8,128)(2,1)S(1)} %get-tuple-element.199), channel_id=1, source_target_pairs={{0,4},{4,8},{8,12},{1,5},{5,9},{9,13},{2,6},{6,10},{10,14},{3,7},{... | collective-permute-start | bytes 23048 | tf_op jit(solution)/shard_map/while/body/eval_jaxpr/ppermute | solution.py:16
  66.6 4.2 %collective-permute-start.1 = (bf16[3,5,16,16]{3,2,1,0:T(8,128)(2,1)S(1)}, bf16[3,5,16,16]{3,2,1,0:T(8,128)(2,1)S(1)}, u32[]{:S(2)}, u32[]{:S(2)}) collective-permute-start(bf16[3,5,16,16]{3,2,1,0:T(8,128)(2,1)S(1)} %collective-permute-done), channel_id=1, source_target_pairs={{0,1},{1,0},{2,3},{3,2},{4,5},{5,4},{6,7},{7,6},{8,9},{9,8},{10,11... | collective-permute-start | bytes 23048 | tf_op jit(solution)/shard_map/while/body/eval_jaxpr/ppermute | solution.py:52
  70.9 5.8 %collective-permute-start.2 = (bf16[3,5,16,32]{3,2,1,0:T(8,128)(2,1)S(1)}, bf16[3,5,16,32]{3,2,1,0:T(8,128)(2,1)S(1)}, u32[]{:S(2)}, u32[]{:S(2)}) collective-permute-start(bf16[3,5,16,32]{3,2,1,0:T(8,128)(2,1)S(1)} %maximum_select_fusion.2), channel_id=1, source_target_pairs={{0,2},{1,3},{2,0},{3,1},{4,6},{5,7},{6,4},{7,5},{8,10},{9,11},{10,... | collective-permute-start | bytes 46088 | tf_op jit(solution)/shard_map/while/body/eval_jaxpr/ppermute | solution.py:52
  91.1 5.5 %collective-permute-start = (bf16[3,5,16,16]{3,2,1,0:T(8,128)(2,1)S(1)}, bf16[3,5,16,16]{3,2,1,0:T(8,128)(2,1)S(1)}, u32[]{:S(2)}, u32[]{:S(2)}) collective-permute-start(bf16[3,5,16,16]{3,2,1,0:T(8,128)(2,1)S(1)} %get-tuple-element.199), channel_id=1, source_target_pairs={{0,4},{4,8},{8,12},{1,5},{5,9},{9,13},{2,6},{6,10},{10,14},{3,7},{... | collective-permute-start | bytes 23048 | tf_op jit(solution)/shard_map/while/body/eval_jaxpr/ppermute | solution.py:16
  96.6 4.2 %collective-permute-start.1 = (bf16[3,5,16,16]{3,2,1,0:T(8,128)(2,1)S(1)}, bf16[3,5,16,16]{3,2,1,0:T(8,128)(2,1)S(1)}, u32[]{:S(2)}, u32[]{:S(2)}) collective-permute-start(bf16[3,5,16,16]{3,2,1,0:T(8,128)(2,1)S(1)} %collective-permute-done), channel_id=1, source_target_pairs={{0,1},{1,0},{2,3},{3,2},{4,5},{5,4},{6,7},{7,6},{8,9},{9,8},{10,11... | collective-permute-start | bytes 23048 | tf_op jit(solution)/shard_map/while/body/eval_jaxpr/ppermute | solution.py:52
  101.0 5.8 %collective-permute-start.2 = (bf16[3,5,16,32]{3,2,1,0:T(8,128)(2,1)S(1)}, bf16[3,5,16,32]{3,2,1,0:T(8,128)(2,1)S(1)}, u32[]{:S(2)}, u32[]{:S(2)}) collective-permute-start(bf16[3,5,16,32]{3,2,1,0:T(8,128)(2,1)S(1)} %maximum_select_fusion.2), channel_id=1, source_target_pairs={{0,2},{1,3},{2,0},{3,1},{4,6},{5,7},{6,4},{7,5},{8,10},{9,11},{10,... | collective-permute-start | bytes 46088 | tf_op jit(solution)/shard_map/while/body/eval_jaxpr/ppermute | solution.py:52
